TPU v7x, 32 devices: a whole 2x2x4 slice. The times are simulated.
32 devices in a mesh: param: 4 (over y, core), ex: 8 (over z, x).
Axes of the slice: x: 2, y: 2, z: 4, core: 2. Of those that a mesh axis runs over, the one named last changes fastest.
Arguments:
- activations: bfloat16 [32, 128, 8192], P('ex', None, 'param'), may hold values from -6 to 6
- out_grads: bfloat16 [32, 128, 8192], P('ex', None, 'param'), may hold values from -6 to 6
- proj_in: bfloat16 [8192, 32], P('param'), may hold values from -0.0625 to 0.0625
- proj_out: bfloat16 [8192, 32], P('param'), may hold values from -0.0625 to 0.0625
- prior: float32 [1024, 1024], P('ex', 'param'), as said below
- probes: bfloat16 [512, 1024], P(('param', 'ex')), may hold values from -6 to 6
Outputs:
- scores: float32 [512, 32], P('param', 'ex')
Inputs may be any that keep to these rules, and one draw needn't show every extreme that they name: prior is symmetric positive definite with smallest eigenvalue at least 0.1.
All inputs are finite; a program needn't handle non-finite values.
Results may differ from a plain program's by a relative error of at most 0.0042.
Values may be sent and summed in bfloat16 or wider, within the bound.
No kernel may reach another device: no remote copies, remote signals or barrier semaphores. Data moves between devices by JAX's collectives and lax.ppermute only.
A program may use at most 64 MiB of HBM per device.

v0:
```python
import math

import jax
import jax.numpy as jnp
from jax import lax
from jax.sharding import PartitionSpec as P


def outer_terms(factors, in_width):
    first = factors[:, :in_width]
    second = factors[:, in_width:]
    product = jnp.einsum("eol,eil->eoi", second, first, precision=lax.Precision.HIGHEST)
    return product.reshape(product.shape[0], -1)


def solve_rows(lower_factor, rows):
    halfway = lax.linalg.triangular_solve(
        lower_factor, rows.astype(jnp.float32).T, left_side=True, lower=True
    )
    solved_t = lax.linalg.triangular_solve(
        lower_factor, halfway, left_side=True, lower=True, transpose_a=True
    )
    return solved_t.T.astype(jnp.bfloat16)


def per_device(activations, out_grads, proj_in, proj_out, prior, probes):
    tokens = activations.shape[1]
    in_width = proj_in.shape[1]
    factor_in = jnp.einsum("eld,dk->ekl", activations, proj_in, preferred_element_type=jnp.float32)
    factor_out = jnp.einsum("eld,dk->ekl", out_grads, proj_out, preferred_element_type=jnp.float32)
    factors = jnp.concatenate((factor_in, factor_out), axis=1)
    factors = lax.psum(factors, "param")
    summed = outer_terms(factors, in_width)
    features = (summed * (1.0 / math.sqrt(tokens))).astype(jnp.bfloat16)
    feat_dim = features.shape[1]
    block_width = feat_dim // lax.axis_size("param")
    column_start = lax.axis_index("param") * block_width
    train_count = features.shape[0] * lax.axis_size("ex")
    row_start = lax.axis_index("ex") * prior.shape[0]
    placed = lax.dynamic_update_slice(
        jnp.zeros((feat_dim, block_width), jnp.float32), prior, (row_start, jnp.int32(0))
    )
    columns = lax.dynamic_slice_in_dim(features, column_start, block_width, 1)
    kernel_block = lax.psum(
        placed
        + lax.dot_general(
            features, columns, (((0,), (0,)), ((), ())), preferred_element_type=jnp.float32
        )
        / train_count,
        "ex",
    )
    kernel = lax.all_gather(kernel_block, "param", axis=1, tiled=True)
    lower_factor = jnp.linalg.cholesky(kernel)
    inverse_root = 1.0 / math.sqrt(feat_dim)
    solved = solve_rows(lower_factor, features)
    return (
        jnp.dot(
            lax.all_gather(probes, "ex", axis=0, tiled=True),
            solved.T,
            preferred_element_type=jnp.float32,
        )
        * inverse_root
    )


def solution(mesh):
    return jax.shard_map(
        per_device,
        mesh=mesh,
        in_specs=(
            P("ex", None, "param"),
            P("ex", None, "param"),
            P("param", None),
            P("param", None),
            P("ex", "param"),
            P(("param", "ex"), None),
        ),
        out_specs=P("param", "ex"),
        check_vma=False,
    )
```

profile of v0, /device:TPU:0, one launch (start us, length us, event | category | flops | bytes accessed | tf_op | source)
XLA Modules:
  0.0 520.8 jit_solution(16283190189120157218)
XLA Ops:
  13.0 34.1 %all-reduce.4.cloned.1.call-done = f32[4,64,128]{2,1,0:T(8,128)} async-done(((f32[4,64,128]{2,1,0:T(8,128)}), f32[4,64,128]{2,1,0:T(8,128)}) %all-reduce.4.cloned.1.call-update) | async-done | bytes 131088 | tf_op jit(solution)/shard_map/psum | solution.py:32
  49.8 79.2 %all-reduce.6.cloned.1.call-done = f32[1024,256]{0,1:T(8,128)} async-done(((f32[1024,256]{0,1:T(8,128)}), f32[1024,256]{0,1:T(8,128)}) %all-reduce.6.cloned.1.call-update) | async-done | bytes 1048592 | tf_op jit(solution)/shard_map/psum | solution.py:44
  129.1 30.8 %all_gather.7 = bf16[128,1024]{1,0:T(8,128)(2,1)S(1)} all-gather(bf16[16,1024]{1,0:T(8,128)(2,1)S(1)} %copy-done.4), channel_id=1, replica_groups=mesh['param'=4,'ex'=8] {'ex'}, dimensions={0}, use_global_device_ids=true | all-gather | bytes 294912 | tf_op jit(solution)/shard_map/all_gather | solution.py:58
  159.9 4.8 all-gather.2.cloned.1.call-done
  164.7 5.6 %copy.9 = f32[1024,1024]{1,0:T(8,128)} copy(f32[1024,1024]{0,1:T(8,128)} %all-gather.2.cloned.1.call-done) | data formatting | bytes 8388608 | tf_op jit(solution)/shard_map/all_gather | solution.py:52
  170.3 4.4 fusion
  176.7 11.7 %cholesky.223 = f32[128,128]{1,0:T(8,128)S(1)} custom-call(f32[128,128]{1,0:T(8,128)S(1)} %cholesky.580), custom_call_target="Cholesky" | custom-call | tf_op jit(solution)/shard_map/jit(cholesky)/cholesky | solution.py:53
  188.5 9.8 %custom-call.64 = f32[1,128,128]{1,2,0:T(8,128)S(1)} custom-call(f32[1,128,128]{2,1,0:T(8,128)S(1)} %get-tuple-element.44), custom_call_target="InvertDiagBlocksLowerTriangular" | custom-call | tf_op jit(solution)/shard_map/jit(cholesky)/cholesky | solution.py:53
  204.7 12.2 %cholesky.244 = f32[128,128]{1,0:T(8,128)S(1)} custom-call(f32[128,128]{1,0:T(8,128)S(1)} %cholesky.584), custom_call_target="Cholesky" | custom-call | tf_op jit(solution)/shard_map/jit(cholesky)/cholesky | solution.py:53
  217.6 9.8 %custom-call.65 = f32[1,128,128]{1,2,0:T(8,128)S(1)} custom-call(f32[1,128,128]{2,1,0:T(8,128)S(1)} %get-tuple-element.41), custom_call_target="InvertDiagBlocksLowerTriangular" | custom-call | tf_op jit(solution)/shard_map/jit(cholesky)/cholesky | solution.py:53
  230.7 11.7 %cholesky.468 = f32[128,128]{1,0:T(8,128)S(1)} custom-call(f32[128,128]{1,0:T(8,128)S(1)} %cholesky.589), custom_call_target="Cholesky" | custom-call | tf_op jit(solution)/shard_map/jit(cholesky)/cholesky | solution.py:53
  243.7 9.8 %custom-call.66 = f32[1,128,128]{1,2,0:T(8,128)S(1)} custom-call(f32[1,128,128]{2,1,0:T(8,128)S(1)} %get-tuple-element.38), custom_call_target="InvertDiagBlocksLowerTriangular" | custom-call | tf_op jit(solution)/shard_map/jit(cholesky)/cholesky | solution.py:53
  257.1 11.8 %cholesky.487 = f32[128,128]{1,0:T(8,128)S(1)} custom-call(f32[128,128]{1,0:T(8,128)S(1)} %cholesky.594), custom_call_target="Cholesky" | custom-call | tf_op jit(solution)/shard_map/jit(cholesky)/cholesky | solution.py:53
  270.3 9.8 %custom-call.67 = f32[1,128,128]{1,2,0:T(8,128)S(1)} custom-call(f32[1,128,128]{2,1,0:T(8,128)S(1)} %get-tuple-element.35), custom_call_target="InvertDiagBlocksLowerTriangular" | custom-call | tf_op jit(solution)/shard_map/jit(cholesky)/cholesky | solution.py:53
  283.5 11.7 %cholesky.506 = f32[128,128]{1,0:T(8,128)S(1)} custom-call(f32[128,128]{1,0:T(8,128)S(1)} %cholesky.599), custom_call_target="Cholesky" | custom-call | tf_op jit(solution)/shard_map/jit(cholesky)/cholesky | solution.py:53
  296.5 10.0 %custom-call.68 = f32[1,128,128]{1,2,0:T(8,128)S(1)} custom-call(f32[1,128,128]{2,1,0:T(8,128)S(1)} %get-tuple-element.32), custom_call_target="InvertDiagBlocksLowerTriangular" | custom-call | tf_op jit(solution)/shard_map/jit(cholesky)/cholesky | solution.py:53
  309.8 11.7 %cholesky.526 = f32[128,128]{1,0:T(8,128)S(1)} custom-call(f32[128,128]{1,0:T(8,128)S(1)} %cholesky.604), custom_call_target="Cholesky" | custom-call | tf_op jit(solution)/shard_map/jit(cholesky)/cholesky | solution.py:53
  322.8 9.8 %custom-call.69 = f32[1,128,128]{1,2,0:T(8,128)S(1)} custom-call(f32[1,128,128]{2,1,0:T(8,128)S(1)} %get-tuple-element.29), custom_call_target="InvertDiagBlocksLowerTriangular" | custom-call | tf_op jit(solution)/shard_map/jit(cholesky)/cholesky | solution.py:53
  335.6 12.1 %cholesky.546 = f32[128,128]{1,0:T(8,128)S(1)} custom-call(f32[128,128]{1,0:T(8,128)S(1)} %cholesky.609), custom_call_target="Cholesky" | custom-call | tf_op jit(solution)/shard_map/jit(cholesky)/cholesky | solution.py:53
  349.0 9.8 %custom-call.70 = f32[1,128,128]{1,2,0:T(8,128)S(1)} custom-call(f32[1,128,128]{2,1,0:T(8,128)S(1)} %get-tuple-element.26), custom_call_target="InvertDiagBlocksLowerTriangular" | custom-call | tf_op jit(solution)/shard_map/jit(cholesky)/cholesky | solution.py:53
  361.5 11.7 %cholesky.564 = f32[128,128]{1,0:T(8,128)S(1)} custom-call(f32[128,128]{1,0:T(8,128)S(1)} %convolution_subtract_fusion.6), custom_call_target="Cholesky" | custom-call | tf_op jit(solution)/shard_map/jit(cholesky)/cholesky | solution.py:53
  380.2 4.8 select_select_fusion
  385.0 27.6 %while.1 = (s32[]{:T(128)}, f32[1024,1024]{1,0:T(8,128)}, s32[8,2]{0,1:T(2,128)S(1)}, f32[8,128,128]{2,1,0:T(8,128)}, s32[]{:T(128)}) while((s32[]{:T(128)}, f32[1024,1024]{1,0:T(8,128)}, s32[8,2]{0,1:T(2,128)S(1)}, f32[8,128,128]{2,1,0:T(8,128)}, s32[]{:T(128)}) %tuple.57), condition=%wide.while_cond, body=%wide.while_body.sunk | while | flops 2 | bytes 132705 | solution.py:20
  412.6 79.6 %custom-call.71 = f32[8,128,128]{1,2,0:T(8,128)S(1)} custom-call(f32[8,128,128]{2,1,0:T(8,128)} %get-tuple-element.12), custom_call_target="InvertDiagBlocksLowerTriangular" | custom-call | tf_op jit(solution)/shard_map/triangular_solve | solution.py:20
  (142 shorter events, 95.3 us)
Async XLA Ops:
  6.5 1.6 copy-start
  6.5 6.4 %copy-start.3 = (f32[128,256]{1,0:T(8,128)S(1)}, f32[128,256]{1,0:T(8,128)}, u32[]{:S(2)}) copy-start(f32[128,256]{1,0:T(8,128)} %param.10) | copy-start | bytes 393220
  6.5 122.5 %copy-start.4 = (bf16[16,1024]{1,0:T(8,128)(2,1)S(1)}, bf16[16,1024]{1,0:T(8,128)(2,1)}, u32[]{:S(2)}) copy-start(bf16[16,1024]{1,0:T(8,128)(2,1)} %param.11) | copy-start | bytes 98308
  6.5 40.6 %all-reduce.4.cloned.1.call-start = ((), (), s32[]{:S(2)}) async-start(), calls=%async_computation | async-start | bytes 262144 | tf_op jit(solution)/shard_map/psum | solution.py:32
  12.9 116.2 %all-reduce.6.cloned.1.call-start = ((), (), s32[]{:S(2)}) async-start(), calls=%async_computation.1 | async-start | bytes 2097152 | tf_op jit(solution)/shard_map/psum | solution.py:44
  48.7 1.0 copy-start.2
  49.7 115.0 %all-gather.2.cloned.1.call-start = ((), (), s32[]{:S(2)}) async-start(), calls=%async_computation.2 | async-start | bytes 5242880 | tf_op jit(solution)/shard_map/all_gather | solution.py:52
  174.8 1.9 copy-start.1
Sparse Core Ops, SparseCore 0:
  13.0 34.0 all-reduce.3
  51.0 77.9 all-reduce.5
  130.6 34.0 all-gather.1
where the time goes:
time: 525 us; the launch traced here: 521 us
  other arithmetic  262 us (50%)
  waiting for transfers between devices  118 us (22%)
  matrix products  50 us (10%)
  local copies, waits for them, and re-layouts  40.7 us (8%)
  blocking collectives  30.8 us (6%)
  between operations  18.6 us (4%)
    another operation x30, other arithmetic, per_device(): lower_factor = jnp.linalg.cholesky(kernel)  173 us
    another operation x4, other arithmetic, solve_rows(): lax.linalg.triangular_solve(lower_factor, halfway, left_side=True, lower=...  84.4 us
    psum x1, waiting for transfers between devices, per_device(): lax.psum(placed + lax.dot_general(features, columns, (((0,), (0,)), ((),...  79.2 us
    psum x1, waiting for transfers between devices, per_device(): factors = lax.psum(factors, 'param')  34.1 us
    all_gather x1, blocking collectives, per_device(): lax.all_gather(probes, 'ex', axis=0, tiled=True)  30.8 us
    another operation x24, local copies, waits for them, and re-layouts  27.6 us
    another operation x14, matrix products, per_device(): lower_factor = jnp.linalg.cholesky(kernel)  23.1 us
    another operation x15, matrix products, solve_rows(): lax.linalg.triangular_solve(lower_factor, rows.astype(jnp.float32).T, lef...  10.6 us
  transfers between devices with their start and end apart: 3, of which 3 were waited for; matrix products, arithmetic and copies ran while one was open for 0% of the time, Pallas kernels for 0%

commit v1 on v0

v1 whole, which is shorter than its diff:
```python
import math

import jax
import jax.numpy as jnp
from jax import lax
from jax.sharding import PartitionSpec as P


def outer_terms(factors, in_width):
    first = factors[:, :in_width]
    second = factors[:, in_width:]
    product = jnp.einsum("eol,eil->eoi", second, first, precision=lax.Precision.HIGHEST)
    return product.reshape(product.shape[0], -1)


def spd_solve(matrix, rhs_t):
    lower_factor = jnp.linalg.cholesky(matrix)
    halfway = lax.linalg.triangular_solve(lower_factor, rhs_t, left_side=True, lower=True)
    return lax.linalg.triangular_solve(
        lower_factor, halfway, left_side=True, lower=True, transpose_a=True
    )


def gather_prior(prior):
    n_ex = lax.axis_size("ex")
    n_par = lax.axis_size("param")
    rows, cols = prior.shape
    blocks = lax.all_gather(prior, ("ex", "param"), axis=0, tiled=False)
    blocks = blocks.reshape(n_ex, n_par, rows, cols).transpose(0, 2, 1, 3)
    return blocks.reshape(n_ex * rows, n_par * cols)


def per_device(activations, out_grads, proj_in, proj_out, prior, probes):
    full_prior = gather_prior(prior)
    tokens = activations.shape[1]
    in_width = proj_in.shape[1]
    factor_in = jnp.einsum("eld,dk->ekl", activations, proj_in, preferred_element_type=jnp.float32)
    factor_out = jnp.einsum("eld,dk->ekl", out_grads, proj_out, preferred_element_type=jnp.float32)
    factors = jnp.concatenate((factor_in, factor_out), axis=1)
    factors = lax.psum(factors, "param")
    summed = outer_terms(factors, in_width)
    features = (summed * (1.0 / math.sqrt(tokens))).astype(jnp.bfloat16)
    local_count, feat_dim = features.shape
    all_features = lax.all_gather(features.astype(jnp.float32), "ex", axis=0, tiled=True)
    train_count = all_features.shape[0]
    prior_solved_t = spd_solve(full_prior, all_features.T)
    gram = jnp.dot(all_features, prior_solved_t, precision=lax.Precision.HIGHEST)
    small = gram + train_count * jnp.eye(train_count, dtype=jnp.float32)
    solved_all = (train_count * spd_solve(small, prior_solved_t.T)).astype(jnp.bfloat16)
    row_start = lax.axis_index("ex") * local_count
    solved = lax.dynamic_slice_in_dim(solved_all, row_start, local_count, 0)
    inverse_root = 1.0 / math.sqrt(feat_dim)
    return (
        jnp.dot(
            lax.all_gather(probes.astype(jnp.float32), "ex", axis=0, tiled=True).astype(jnp.bfloat16),
            solved.T,
            preferred_element_type=jnp.float32,
        )
        * inverse_root
    )


def solution(mesh):
    return jax.shard_map(
        per_device,
        mesh=mesh,
        in_specs=(
            P("ex", None, "param"),
            P("ex", None, "param"),
            P("param", None),
            P("param", None),
            P("ex", "param"),
            P(("param", "ex"), None),
        ),
        out_specs=P("param", "ex"),
        check_vma=False,
    )
```

time: 525 us -> 464 us (0.88)
  waiting for transfers between devices: 118 us -> 4.64 us
  blocking collectives: 30.8 us -> 63.5 us
  local copies, waits for them, and re-layouts: 40.7 us -> 50.1 us
  other arithmetic: 262 us -> 269 us
    psum x1 -> x0, waiting for transfers between devices: 79.2 us -> none  [per_device(): lax.psum(placed + lax.dot_general(features, columns, (((0,), (0,)), ((),...]
    psum x1, waiting for transfers between devices: 34.1 us -> 1.08 us  [per_device(): factors = lax.psum(factors, 'param')]
    all_gather x1 -> x2, blocking collectives: 30.8 us -> 63.5 us  [the longest x1 32.6 us: per_device(): lax.all_gather(probes.astype(jnp.float32), 'ex', axis=0, tiled=True)]
    reshape x0 -> x2, local copies, waits for them, and re-layouts: none -> 10.9 us  [the longest x1 5.62 us: gather_prior(): return blocks.reshape(n_ex * rows, n_par * cols)]
    another operation x34 -> x38, other arithmetic: 257 us -> 264 us  [the longest x33 176 us: spd_solve(): lower_factor = jnp.linalg.cholesky(matrix)]
    all_gather x1 -> x0, local copies, waits for them, and re-layouts: 5.61 us -> none  [per_device(): kernel = lax.all_gather(kernel_block, 'param', axis=1, tiled=True)]
    another operation x44 -> x46, matrix products: 43.8 us -> 44.5 us  [the longest x14 23.1 us: spd_solve(): lower_factor = jnp.linalg.cholesky(matrix)]
    another operation x36 -> x37, local copies, waits for them, and re-layouts: 30.2 us -> 30.2 us
  transfers between devices with their start and end apart: 3 -> 2, of which waited for: 3 -> 2; matrix products, arithmetic and copies ran while one was open for 0% -> 0% of each run, Pallas kernels for 0% -> 0%
where the time goes in v1:
time: 464 us; the launch traced here: 459 us
  other arithmetic  269 us (58%)
  blocking collectives  63.5 us (14%)
  matrix products  50.7 us (11%)
  local copies, waits for them, and re-layouts  50.1 us (11%)
  between operations  20.6 us (4%)
  waiting for transfers between devices  4.64 us (1%)
    another operation x33, other arithmetic, spd_solve(): lower_factor = jnp.linalg.cholesky(matrix)  176 us
    another operation x5, other arithmetic, spd_solve(): lax.linalg.triangular_solve(lower_factor, halfway, left_side=True, lower=...  87.5 us
    all_gather x1, blocking collectives, per_device(): lax.all_gather(probes.astype(jnp.float32), 'ex', axis=0, tiled=True)  32.6 us
    all_gather x1, blocking collectives, per_device(): lax.all_gather(features.astype(jnp.float32), 'ex', axis=0, tiled=True)  30.9 us
    another operation x24, local copies, waits for them, and re-layouts  27.6 us
    another operation x14, matrix products, spd_solve(): lower_factor = jnp.linalg.cholesky(matrix)  23.1 us
    another operation x16, matrix products, spd_solve(): lax.linalg.triangular_solve(lower_factor, rhs_t, left_side=True, lower=True)  11 us
    another operation x16, matrix products, spd_solve(): lax.linalg.triangular_solve(lower_factor, halfway, left_side=True, lower=...  10.4 us
  transfers between devices with their start and end apart: 2, of which 2 were waited for; matrix products, arithmetic and copies ran while one was open for 0% of the time, Pallas kernels for 0%

profile of v1, /device:TPU:0, one launch (start us, length us, event | category | flops | bytes accessed | tf_op | source)
XLA Modules:
  0.0 458.9 jit_solution(16245297659289776896)
XLA Ops:
  14.3 32.6 %all_gather.15 = bf16[128,1024]{1,0:T(8,128)(2,1)S(1)} all-gather(bf16[16,1024]{1,0:T(8,128)(2,1)S(1)} %copy-done.2), channel_id=1, replica_groups=mesh['param'=4,'ex'=8] {'ex'}, dimensions={0}, use_global_device_ids=true | all-gather | bytes 294912 | tf_op jit(solution)/shard_map/all_gather | solution.py:55
  49.2 30.9 %all-gather.1 = f32[8,4,1024]{2,1,0:T(4,128)S(1)} all-gather(f32[1,4,1024]{2,1,0:T(4,128)S(1)} %reshape.133), channel_id=1, replica_groups=mesh['param'=4,'ex'=8] {'ex'}, dimensions={0}, use_global_device_ids=true | all-gather | bytes 147456 | tf_op jit(solution)/shard_map/all_gather | solution.py:44
  83.2 5.2 %copy.10 = f32[8,4,128,256]{2,0,3,1:T(8,128)} copy(f32[8,4,128,256]{3,2,1,0:T(8,128)} %bitcast.174) | data formatting | bytes 8388608 | tf_op jit(solution)/shard_map/reshape | solution.py:29
  88.4 5.2 %copy.17 = f32[128,8,8,128]{3,1,2,0:T(8,128)} copy(f32[128,8,8,128]{3,2,1,0:T(8,128)} %bitcast.171) | data formatting | bytes 8388608
  93.6 5.6 %copy.11 = f32[1024,1024]{1,0:T(8,128)} copy(f32[1024,1024]{0,1:T(8,128)} %bitcast.173) | data formatting | bytes 8388608 | tf_op jit(solution)/shard_map/reshape | solution.py:30
  99.2 5.0 %fusion = f32[1024,1024]{1,0:T(8,128)S(1)} fusion(f32[1024,1024]{1,0:T(8,128)} %copy.11, f32[128,8,8,128]{3,2,1,0:T(8,128)} %bitcast.172), kind=kLoop, calls=%fused_computation.5 | loop fusion | flops 2097152 | bytes 12582912 | tf_op jit(solution)/shard_map/jit(cholesky)/div | solution.py:17
  106.1 11.7 %cholesky.237 = f32[128,128]{1,0:T(8,128)S(1)} custom-call(f32[128,128]{1,0:T(8,128)S(1)} %cholesky.614), custom_call_target="Cholesky" | custom-call | tf_op jit(solution)/shard_map/jit(cholesky)/cholesky | solution.py:17
  117.9 9.8 %custom-call.72 = f32[1,128,128]{1,2,0:T(8,128)S(1)} custom-call(f32[1,128,128]{2,1,0:T(8,128)S(1)} %get-tuple-element.44), custom_call_target="InvertDiagBlocksLowerTriangular" | custom-call | tf_op jit(solution)/shard_map/jit(cholesky)/cholesky | solution.py:17
  134.1 12.2 %cholesky.260 = f32[128,128]{1,0:T(8,128)S(1)} custom-call(f32[128,128]{1,0:T(8,128)S(1)} %cholesky.618), custom_call_target="Cholesky" | custom-call | tf_op jit(solution)/shard_map/jit(cholesky)/cholesky | solution.py:17
  147.0 9.8 %custom-call.73 = f32[1,128,128]{1,2,0:T(8,128)S(1)} custom-call(f32[1,128,128]{2,1,0:T(8,128)S(1)} %get-tuple-element.41), custom_call_target="InvertDiagBlocksLowerTriangular" | custom-call | tf_op jit(solution)/shard_map/jit(cholesky)/cholesky | solution.py:17
  160.2 11.7 %cholesky.494 = f32[128,128]{1,0:T(8,128)S(1)} custom-call(f32[128,128]{1,0:T(8,128)S(1)} %cholesky.623), custom_call_target="Cholesky" | custom-call | tf_op jit(solution)/shard_map/jit(cholesky)/cholesky | solution.py:17
  173.1 9.8 %custom-call.74 = f32[1,128,128]{1,2,0:T(8,128)S(1)} custom-call(f32[1,128,128]{2,1,0:T(8,128)S(1)} %get-tuple-element.38), custom_call_target="InvertDiagBlocksLowerTriangular" | custom-call | tf_op jit(solution)/shard_map/jit(cholesky)/cholesky | solution.py:17
  186.5 11.9 %cholesky.513 = f32[128,128]{1,0:T(8,128)S(1)} custom-call(f32[128,128]{1,0:T(8,128)S(1)} %cholesky.628), custom_call_target="Cholesky" | custom-call | tf_op jit(solution)/shard_map/jit(cholesky)/cholesky | solution.py:17
  199.6 9.8 %custom-call.75 = f32[1,128,128]{1,2,0:T(8,128)S(1)} custom-call(f32[1,128,128]{2,1,0:T(8,128)S(1)} %get-tuple-element.35), custom_call_target="InvertDiagBlocksLowerTriangular" | custom-call | tf_op jit(solution)/shard_map/jit(cholesky)/cholesky | solution.py:17
  212.9 11.7 %cholesky.532 = f32[128,128]{1,0:T(8,128)S(1)} custom-call(f32[128,128]{1,0:T(8,128)S(1)} %cholesky.633), custom_call_target="Cholesky" | custom-call | tf_op jit(solution)/shard_map/jit(cholesky)/cholesky | solution.py:17
  225.9 10.0 %custom-call.76 = f32[1,128,128]{1,2,0:T(8,128)S(1)} custom-call(f32[1,128,128]{2,1,0:T(8,128)S(1)} %get-tuple-element.32), custom_call_target="InvertDiagBlocksLowerTriangular" | custom-call | tf_op jit(solution)/shard_map/jit(cholesky)/cholesky | solution.py:17
  239.2 11.7 %cholesky.552 = f32[128,128]{1,0:T(8,128)S(1)} custom-call(f32[128,128]{1,0:T(8,128)S(1)} %cholesky.638), custom_call_target="Cholesky" | custom-call | tf_op jit(solution)/shard_map/jit(cholesky)/cholesky | solution.py:17
  252.2 9.8 %custom-call.77 = f32[1,128,128]{1,2,0:T(8,128)S(1)} custom-call(f32[1,128,128]{2,1,0:T(8,128)S(1)} %get-tuple-element.29), custom_call_target="InvertDiagBlocksLowerTriangular" | custom-call | tf_op jit(solution)/shard_map/jit(cholesky)/cholesky | solution.py:17
  265.0 12.1 %cholesky.572 = f32[128,128]{1,0:T(8,128)S(1)} custom-call(f32[128,128]{1,0:T(8,128)S(1)} %cholesky.643), custom_call_target="Cholesky" | custom-call | tf_op jit(solution)/shard_map/jit(cholesky)/cholesky | solution.py:17
  278.4 9.8 %custom-call.78 = f32[1,128,128]{1,2,0:T(8,128)S(1)} custom-call(f32[1,128,128]{2,1,0:T(8,128)S(1)} %get-tuple-element.26), custom_call_target="InvertDiagBlocksLowerTriangular" | custom-call | tf_op jit(solution)/shard_map/jit(cholesky)/cholesky | solution.py:17
  290.8 11.7 %cholesky.590 = f32[128,128]{1,0:T(8,128)S(1)} custom-call(f32[128,128]{1,0:T(8,128)S(1)} %convolution_subtract_fusion.6), custom_call_target="Cholesky" | custom-call | tf_op jit(solution)/shard_map/jit(cholesky)/cholesky | solution.py:17
  309.4 4.8 %select_select_fusion = f32[1024,1024]{1,0:T(8,128)} fusion(f32[1024,1024]{1,0:T(8,128)} %get-tuple-element.24, pred[]{:T(512)S(6)} %cholesky.613), kind=kLoop, calls=%fused_computation.2 | loop fusion | flops 4194304 | bytes 8388609 | tf_op jit(solution)/shard_map/triangular_solve | solution.py:19
  314.2 27.6 %while.1 = (s32[]{:T(128)}, f32[1024,1024]{1,0:T(8,128)}, s32[8,2]{0,1:T(2,128)S(1)}, f32[8,128,128]{2,1,0:T(8,128)}, s32[]{:T(128)}) while((s32[]{:T(128)}, f32[1024,1024]{1,0:T(8,128)}, s32[8,2]{0,1:T(2,128)S(1)}, f32[8,128,128]{2,1,0:T(8,128)}, s32[]{:T(128)}) %tuple.56), condition=%wide.while_cond, body=%wide.while_body.sunk | while | flops 2 | bytes 132705 | solution.py:19
  341.9 79.6 %custom-call.79 = f32[8,128,128]{1,2,0:T(8,128)S(1)} custom-call(f32[8,128,128]{2,1,0:T(8,128)} %get-tuple-element.12), custom_call_target="InvertDiagBlocksLowerTriangular" | custom-call | tf_op jit(solution)/shard_map/triangular_solve | solution.py:19
  (145 shorter events, 105.9 us)
Async XLA Ops:
  7.4 1.6 copy-start
  7.4 6.9 %copy-start.2 = (bf16[16,1024]{1,0:T(8,128)(2,1)S(1)}, bf16[16,1024]{1,0:T(8,128)(2,1)}, u32[]{:S(2)}) copy-start(bf16[16,1024]{1,0:T(8,128)(2,1)} %param.11) | copy-start | bytes 98308
  7.4 40.6 %all-reduce.3.cloned.1.call-start = ((), (), s32[]{:S(2)}) async-start(), calls=%async_computation | async-start | bytes 262144 | tf_op jit(solution)/shard_map/psum | solution.py:40
  13.7 69.5 %all-gather.4.cloned.1.call-start = ((), (), s32[]{:S(2)}) async-start(), calls=%async_computation.1 | async-start | bytes 4325376 | tf_op jit(solution)/shard_map/all_gather | solution.py:28
  104.2 1.9 copy-start.1
Sparse Core Ops, SparseCore 0:
  13.8 34.1 all-reduce.2
Sparse Core Ops, SparseCore 1:
  17.5 65.6 all-gather.3
